TPU v7x, 512 devices: a whole 4x4x16 slice. The times are simulated.
512 devices in a mesh: dp: 32 (over z, core), expert: 16 (over x, y).
Axes of the slice: x: 4, y: 4, z: 16, core: 2. Of those that a mesh axis runs over, the one named last changes fastest.
Arguments:
- grad_out: bfloat16 [65536, 2048], P(('dp', 'expert')), may hold values from -6 to 6
- gate: float32 [65536, 1], P(('dp', 'expert')), may hold values from 0.25 to 1
- expert_ids: int32 [65536, 1], P(('dp', 'expert')), may hold values from 0 to 15; in each aligned block of 128 rows (0 to 127, 128 to 255, ...) at most 10 rows name the same one
- w_in: bfloat16 [16, 5120, 2048], P('expert', 'dp'), may hold values from -0.125 to 0.125
- w_out: bfloat16 [16, 5120, 2048], P('expert', 'dp'), may hold values from -0.078125 to 0.078125
- pre_act: bfloat16 [32, 16, 160, 5120], P('dp', 'expert'), may hold values from -6 to 6
Outputs:
- grad_in: bfloat16 [65536, 2048], P(('dp', 'expert'))
Inputs may be any that keep to these rules, and one draw needn't show every extreme that they name: `expert_ids`: among the 128 tokens of one device no expert is named more than 10 times, and in every draw some device names some expert exactly 10 times.
All inputs are finite; a program needn't handle non-finite values.
Results may differ from a plain program's by a relative error of at most 0.0057.
Values may be sent and summed in bfloat16 or wider, within the bound.
No kernel may reach another device: no remote copies, remote signals or barrier semaphores. Data moves between devices by JAX's collectives and lax.ppermute only.
A program may use at most 192 MiB of HBM per device.

v0:
```python
import jax
import jax.numpy as jnp
from jax import lax
from jax.sharding import PartitionSpec as P


def gelu_slope(values):
    inside = 0.7978845608028654 * (values + 0.044715 * values * values * values)
    curved = jnp.tanh(inside)
    return 0.5 * (1.0 + curved) + 0.5 * values * (1.0 - curved * curved) * 0.7978845608028654 * (
        1.0 + 3.0 * 0.044715 * values * values
    )


def body(grad_out, gate, expert_ids, w_in, w_out, pre_act):
    groups = lax.axis_size("expert")
    slots = pre_act.shape[2]
    capacity = slots // groups
    width = grad_out.shape[1]
    chosen = expert_ids[:, 0]
    hit_table = (chosen[:, None] == jnp.arange(groups, dtype=jnp.int32)[None, :]).astype(jnp.int32)
    position = jnp.sum(jnp.cumsum(hit_table, axis=0) * hit_table, axis=1) - 1
    target = chosen * capacity + position
    scaled = (grad_out.astype(jnp.float32) * gate).astype(jnp.bfloat16)
    outgoing = (
        jnp.zeros((slots, width), jnp.bfloat16)
        .at[target]
        .set(scaled)
        .reshape(groups, capacity, width)
    )
    arrived = lax.all_to_all(outgoing, "expert", split_axis=0, concat_axis=0, tiled=True)
    rows_in = arrived.reshape(slots, width)
    stashed = pre_act[0, 0]
    shards = lax.axis_size("dp")
    rows = w_out.shape[1]
    both = jnp.concatenate([w_out, w_in], axis=1)
    gathered = lax.all_gather(both, "dp", axis=1, tiled=True).reshape(shards, 2, rows, width)
    hidden_grad = jnp.einsum(
        "sd,gfd->sgf", rows_in, gathered[:, 0], preferred_element_type=jnp.float32
    ).reshape(slots, shards * rows)
    act_grad = (hidden_grad * gelu_slope(stashed.astype(jnp.float32))).astype(jnp.bfloat16)
    slot_sum = jnp.einsum(
        "sgf,gfd->sd",
        act_grad.reshape(slots, shards, rows),
        gathered[:, 1],
        preferred_element_type=jnp.float32,
    )
    slot_grad = slot_sum.astype(jnp.bfloat16).reshape(groups, capacity, width)
    returned = lax.all_to_all(slot_grad, "expert", split_axis=0, concat_axis=0, tiled=True)
    return returned.reshape(slots, width)[target]


def solution(mesh):
    return jax.shard_map(
        body,
        mesh=mesh,
        in_specs=(
            P(("dp", "expert"), None),
            P(("dp", "expert"), None),
            P(("dp", "expert"), None),
            P("expert", "dp", None),
            P("expert", "dp", None),
            P("dp", "expert", None, None),
        ),
        out_specs=P(("dp", "expert"), None),
        check_vma=False,
    )
```

profile of v0, /device:TPU:8, one launch (start us, length us, event | category | flops | bytes accessed | tf_op | source)
XLA Modules:
  0.0 328.3 jit_solution(9330431443200145467)
XLA Ops:
  6.5 0.0 copy-start.1
  6.5 0.0 copy-start.2
  6.5 0.0 copy-start
  6.5 0.0 all-gather.2.cloned.1.call-start
  6.5 2.5 pad_maximum_fusion
  9.1 0.0 all-gather.2.cloned.1.call-update
  9.1 0.0 copy-done.1
  9.1 0.1 fusion.19
  9.2 0.2 reduce_window_sum.11
  9.4 0.2 select_reduce_fusion
  9.6 0.0 copy-done.2
  9.6 0.0 copy-done
  9.6 1.6 scatter_custom_fusion
  11.2 0.2 reshape.32
  11.4 22.9 %all_to_all.10 = bf16[16,10,2048]{2,1,0:T(8,128)(2,1)S(1)} all-to-all(bf16[16,10,2048]{2,1,0:T(8,128)(2,1)S(1)} %reshape.32), channel_id=1, replica_groups=mesh['dp'=32,'expert'=16] {'expert'}, dimensions={0} | all-to-all | bytes 1310720 | tf_op jit(solution)/shard_map/all_to_all | solution.py:31
  34.4 0.2 reshape.33
  34.6 212.7 %all-gather.2.cloned.1.call-done = bf16[1,10240,2048]{2,1,0:T(8,128)(2,1)} async-done(((bf16[1,320,2048]{2,1,0:T(8,128)(2,1)}), bf16[1,10240,2048]{2,1,0:T(8,128)(2,1)}) %all-gather.2.cloned.1.call-update) | async-done | bytes 41943056 | tf_op jit(solution)/shard_map/all_gather | solution.py:37
  247.3 0.0 copy-start.3
  247.3 17.8 %slice.10 = bf16[32,1,160,2048]{3,2,1,0:T(8,128)(2,1)} slice(bf16[32,2,160,2048]{3,2,1,0:T(8,128)(2,1)} %bitcast.29), slice={[0:32], [0:1], [0:160], [0:2048]} | slice | bytes 41943040 | tf_op jit(solution)/shard_map/slice | solution.py:39
  265.0 0.0 copy-done.3
  265.0 13.3 %fusion.1 = bf16[160,5120]{1,0:T(8,128)(2,1)} fusion(bf16[160,2048]{1,0:T(8,128)(2,1)S(1)} %reshape.33, bf16[5120,2048]{1,0:T(8,128)(2,1)} %bitcast.28, bf16[1,1,160,5120]{3,2,1,0:T(8,128)(2,1)S(1)} %copy-done.3), kind=kOutput, calls=%fused_computation.12 | convolution fusion | flops 3371827200 | bytes 24903680 | tf_op jit(solution)/shard_map/sd,gfd->sgf/dot_general | solution.py:38
  278.3 4.4 %reshape.35 = bf16[160,32,160]{2,1,0:T(8,128)(2,1)S(1)} reshape(bf16[160,5120]{1,0:T(8,128)(2,1)} %fusion.1) | data formatting | bytes 3276800 | tf_op jit(solution)/shard_map/reshape | solution.py:44
  282.8 11.4 %fusion.13 = bf16[160,2048]{1,0:T(8,128)(2,1)S(1)} fusion(bf16[32,2,160,2048]{3,2,1,0:T(8,128)(2,1)} %bitcast.30, bf16[160,32,160]{2,1,0:T(8,128)(2,1)S(1)} %reshape.35), kind=kOutput, calls=%fused_computation.22 | convolution fusion | flops 3355770880 | bytes 23265280 | tf_op jit(solution)/shard_map/sgf,gfd->sd/dot_general | solution.py:42
  294.2 1.2 reshape.36
  295.4 7.3 %all-to-all-start.1 = ((bf16[16,10,2048]{2,1,0:T(8,128)(2,1)}), bf16[16,10,2048]{2,1,0:T(8,128)(2,1)S(1)}, u32[]{:S(2)}, u32[]{:S(2)}) async-start(bf16[16,10,2048]{2,1,0:T(8,128)(2,1)} %reshape.36), calls=%async_computation.1 | async-start | bytes 2097152 | tf_op jit(solution)/shard_map/all_to_all | solution.py:49
  302.7 16.8 %all-to-all-done.1 = bf16[16,10,2048]{2,1,0:T(8,128)(2,1)S(1)} async-done(((bf16[16,10,2048]{2,1,0:T(8,128)(2,1)}), bf16[16,10,2048]{2,1,0:T(8,128)(2,1)S(1)}, u32[]{:S(2)}, u32[]{:S(2)}) %all-to-all-start.1) | async-done | bytes 655392 | tf_op jit(solution)/shard_map/all_to_all | solution.py:49
  319.5 0.2 reshape.37
  319.8 1.7 gather_fusion
  (2 shorter events, 0.0 us)
Async XLA Ops:
  6.5 2.6 copy-start.1
  6.5 3.0 copy-start.2
  6.5 3.1 copy-start
  6.5 240.7 %all-gather.2.cloned.1.call-start = ((), (), s32[]{:S(2)}) async-start(), calls=%async_computation.2 | async-start | bytes 43253760 | tf_op jit(solution)/shard_map/all_gather | solution.py:37
  247.3 17.8 %copy-start.3 = (bf16[1,1,160,5120]{3,2,1,0:T(8,128)(2,1)S(1)}, bf16[1,1,160,5120]{3,2,1,0:T(8,128)(2,1)}, u32[]{:S(2)}) copy-start(bf16[1,1,160,5120]{3,2,1,0:T(8,128)(2,1)} %param.11) | copy-start | bytes 4915204
  295.4 24.1 %all-to-all-start.1 = ((bf16[16,10,2048]{2,1,0:T(8,128)(2,1)}), bf16[16,10,2048]{2,1,0:T(8,128)(2,1)S(1)}, u32[]{:S(2)}, u32[]{:S(2)}) async-start(bf16[16,10,2048]{2,1,0:T(8,128)(2,1)} %reshape.36), calls=%async_computation.1 | async-start | bytes 2097152 | tf_op jit(solution)/shard_map/all_to_all | solution.py:49
Sparse Core Ops, SparseCore 0:
  9.5 237.7 all-gather.1
where the time goes:
time: 329 us; the launch traced here: 328 us
  waiting for transfers between devices  230 us (70%)
  local copies, waits for them, and re-layouts  25.8 us (8%)
  matrix products  24.7 us (8%)
  blocking collectives  22.9 us (7%)
  between operations  13.5 us (4%)
  starting transfers between devices  7.26 us (2%)
  other arithmetic  4.6 us (1%)
    all_gather x1, waiting for transfers between devices, body(): lax.all_gather(both, 'dp', axis=1, tiled=True)  213 us
    all_to_all x1, blocking collectives, body(): lax.all_to_all(outgoing, 'expert', split_axis=0, concat_axis=0, tiled=True)  22.9 us
    slice x1, local copies, waits for them, and re-layouts, body(): gathered[:, 0]  17.8 us
    all_to_all x1, waiting for transfers between devices, body(): lax.all_to_all(slot_grad, 'expert', split_axis=0, concat_axis=0, tiled=True)  16.8 us
    dot_general x1, matrix products, body(): jnp.einsum('sd,gfd->sgf', rows_in, gathered[:, 0], preferred_element_type...  13.3 us
    dot_general x1, matrix products, body(): jnp.einsum('sgf,gfd->sd', act_grad.reshape(slots, shards, rows), gathered...  11.4 us
    all_to_all x1, starting transfers between devices, body(): lax.all_to_all(slot_grad, 'expert', split_axis=0, concat_axis=0, tiled=True)  7.26 us
  transfers between devices with their start and end apart: 2, of which 2 were waited for; matrix products, arithmetic and copies ran while one was open for 1% of the time, Pallas kernels for 0%

commit v1 on v0

--- a/solution.py
+++ b/solution.py
@@ -34,7 +34,14 @@
     shards = lax.axis_size("dp")
     rows = w_out.shape[1]
     both = jnp.concatenate([w_out, w_in], axis=1)
-    gathered = lax.all_gather(both, "dp", axis=1, tiled=True).reshape(shards, 2, rows, width)
+
+    def prepare_rounds(mat):
+        kept_arr = jax.lax.all_to_all(
+            jnp.concatenate(jax.lax.axis_size("dp") * [mat], 1), "dp", 1, 1, tiled=True
+        )
+        return kept_arr
+
+    gathered = prepare_rounds(both).reshape(shards, 2, rows, width)
     hidden_grad = jnp.einsum(
         "sd,gfd->sgf", rows_in, gathered[:, 0], preferred_element_type=jnp.float32
     ).reshape(slots, shards * rows)

time: 329 us -> 2500 us (7.60)
  the two profiles are of different devices: /device:TPU:8 before, /device:TPU:32 now
where the time goes in v1:
time: 2500 us; the launch traced here: 2490 us
  waiting for transfers between devices  1820 us (73%)
  local copies, waits for them, and re-layouts  360 us (14%)
  other arithmetic  249 us (10%)
  starting transfers between devices  30 us (1%)
  matrix products  26.4 us (1%)
    all_to_all x1, waiting for transfers between devices, prepare_rounds(): jax.lax.all_to_all(jnp.concatenate(jax.lax.axis_size('dp') * [mat], 1), '...  1810 us
    unnamed x75, local copies, waits for them, and re-layouts  331 us
    unnamed x1, other arithmetic  244 us
  transfers between devices with their start and end apart: 3, of which 2 were waited for; matrix products, arithmetic and copies ran while one was open for 19% of the time, Pallas kernels for 0%

profile of v1, /device:TPU:32, one launch (start us, length us, event | category | flops | bytes accessed | tf_op | source)
XLA Modules:
  0.0 2489.6 jit_solution(2414546131878348559)
XLA Ops:
  5.8 7.0 all-to-all-start
  16.1 3.2 constant_dynamic-update-slice_fusion.62
  19.2 3.2 constant_dynamic-update-slice_fusion.61
  22.4 3.2 constant_dynamic-update-slice_fusion.60
  25.6 3.2 constant_dynamic-update-slice_fusion.59
  32.0 3.3 constant_dynamic-update-slice_fusion.57
  38.4 3.2 constant_dynamic-update-slice_fusion.55
  41.5 3.2 constant_dynamic-update-slice_fusion.54
  47.9 3.5 constant_dynamic-update-slice_fusion.52
  67.2 3.2 constant_dynamic-update-slice_fusion.46
  73.6 3.2 constant_dynamic-update-slice_fusion.44
  83.1 3.4 constant_dynamic-update-slice_fusion.41
  92.8 3.2 constant_dynamic-update-slice_fusion.38
  102.3 3.2 constant_dynamic-update-slice_fusion.35
  108.7 3.2 constant_dynamic-update-slice_fusion.33
  115.0 3.2 constant_dynamic-update-slice_fusion.31
  118.2 3.4 constant_dynamic-update-slice_fusion.30
  124.8 3.2 constant_dynamic-update-slice_fusion.28
  127.9 3.2 constant_dynamic-update-slice_fusion.27
  134.3 3.2 constant_dynamic-update-slice_fusion.25
  191.9 244.4 %reduce = bf16[10240,2048]{1,0:T(8,128)(2,1)} reduce(bf16[10240,1,2048]{2,1,0:T(2,128)(2,1)} %bitcast.26, bf16[]{:T(256)} %broadcast.51), dimensions={1}, to_apply=%bitcast.26.reduce_sub_computation | reduce | bytes 83886080
  436.3 46.7 %reshape.58 = bf16[32,2,327680]{2,1,0:T(2,128)(2,1)} reshape(bf16[10240,2048]{1,0:T(8,128)(2,1)} %reduce) | data formatting | bytes 83886080
  483.0 15.8 all-to-all-start.1
  499.0 1806.9 %all-to-all-done.1 = bf16[32,2,327680]{2,1,0:T(2,128)(2,1)} async-done(((bf16[32,2,327680]{2,1,0:T(2,128)(2,1)}), bf16[32,2,327680]{2,1,0:T(2,128)(2,1)}, u32[]{:S(2)}, u32[]{:S(2)}) %all-to-all-start.1) | async-done | bytes 41943072 | tf_op jit(solution)/shard_map/all_to_all | solution.py:39
  2305.9 57.2 %reshape.59 = bf16[10240,1,2048]{2,1,0:T(2,128)(2,1)} reshape(bf16[32,2,327680]{2,1,0:T(2,128)(2,1)} %all-to-all-done.1) | data formatting | bytes 83886080
  2363.1 50.6 %copy.76 = bf16[1,10240,2048]{2,1,0:T(8,128)(2,1)} copy(bf16[1,10240,2048]{2,0,1:T(2,128)(2,1)} %bitcast.27) | data formatting | bytes 83886080
  2413.7 17.6 slice.10
  2431.3 12.5 fusion.1
  2443.9 4.2 reshape.35
  2448.1 13.9 fusion.13
  2463.1 7.2 all-to-all-start.2
  2470.4 16.8 all-to-all-done.2
  (66 shorter events, 126.8 us)
Async XLA Ops:
  0.0 140.7 %copy-start = (bf16[1,160,2048]{2,1,0:T(8,128)(2,1)S(1)}, bf16[1,160,2048]{2,1,0:T(8,128)(2,1)}, u32[]{:S(2)}) copy-start(bf16[1,160,2048]{2,1,0:T(8,128)(2,1)} %param.10) | copy-start | bytes 1966084
  0.0 142.7 %copy-start.1 = (bf16[1,160,2048]{2,1,0:T(8,128)(2,1)S(1)}, bf16[1,160,2048]{2,1,0:T(8,128)(2,1)}, u32[]{:S(2)}) copy-start(bf16[1,160,2048]{2,1,0:T(8,128)(2,1)} %param.9) | copy-start | bytes 1966084
  2.5 3.3 copy-start.2
  5.8 477.1 %all-to-all-start = ((bf16[16,10,2048]{2,1,0:T(8,128)(2,1)}), bf16[16,10,2048]{2,1,0:T(8,128)(2,1)S(1)}, u32[]{:S(2)}, u32[]{:S(2)}) async-start(bf16[16,10,2048]{2,1,0:T(8,128)(2,1)} %reshape.32), calls=%async_computation | async-start | bytes 2097152 | tf_op jit(solution)/shard_map/all_to_all | solution.py:31
  483.0 1822.9 %all-to-all-start.1 = ((bf16[32,2,327680]{2,1,0:T(2,128)(2,1)}), bf16[32,2,327680]{2,1,0:T(2,128)(2,1)}, u32[]{:S(2)}, u32[]{:S(2)}) async-start(bf16[32,2,327680]{2,1,0:T(2,128)(2,1)} %reshape.58), calls=%async_computation.1 | async-start | bytes 83886080 | tf_op jit(solution)/shard_map/all_to_all | solution.py:39
  2413.7 56.6 %copy-start.3 = (s32[128]{0:T(128)S(1)}, s32[128]{0:T(128)}, u32[]{:S(2)}) copy-start(s32[128]{0:T(128)} %copy-done.2) | copy-start | bytes 1540
  2463.1 24.1 all-to-all-start.2
